TPU v7x, 256 devices: a whole 4x4x8 slice. The times are simulated.
256 devices in a mesh: seq: 8 (over z_hi, core), chan: 16 (over y, x), dp: 2 (over z_lo).
Axes of the slice: x: 4, y: 4, z: 8 (z_hi: 4, z_lo: 2; z = z_hi * 2 + z_lo), core: 2. Of those that a mesh axis runs over, the one named last changes fastest.
Arguments:
- query_proj: bfloat16 [2, 4096, 8192], P('dp', 'seq', 'chan'), may hold values from -6 to 6
- key_proj: bfloat16 [2, 4096, 8192], P('dp', 'seq', 'chan')
- value_proj: bfloat16 [2, 4096, 8192], P('dp', 'seq', 'chan')
- cotangent: bfloat16 [2, 4096, 8192], P('dp', 'seq', 'chan'), may hold values from -6 to 6
- long_filter: float32 [4096, 8192], P('seq', 'chan')
- skip_gain: float32 [8192], P('chan'), may hold values from -3 to 3
Outputs:
- output: bfloat16 [2, 4096, 8192], P('dp', 'seq', 'chan')
- grad_query: bfloat16 [2, 4096, 8192], P('dp', 'seq', 'chan')
- grad_key: bfloat16 [2, 4096, 8192], P('dp', 'seq', 'chan')
- grad_value: bfloat16 [2, 4096, 8192], P('dp', 'seq', 'chan')
- grad_filter: float32 [4096, 8192], P('seq', 'chan')
- grad_skip: float32 [8192], P('chan')
All inputs are finite; a program needn't handle non-finite values.
Results may differ from a plain program's by a relative error of at most 0.0095.
Values may be sent and summed in bfloat16 or wider, within the bound.
No kernel may reach another device: no remote copies, remote signals or barrier semaphores. Data moves between devices by JAX's collectives and lax.ppermute only.
A program may use at most 64 MiB of HBM per device.

v0:
```python
import math
import jax
import jax.numpy as jnp
from jax import lax
from jax.sharding import PartitionSpec as P

full_precision = lax.Precision.HIGHEST


def dft_tables(seq_length):
    full_size = 2 * seq_length
    inner_size = 128
    outer_size = full_size // inner_size
    half_size = outer_size // 2
    outer_index = jnp.arange(outer_size, dtype=jnp.int32)
    half_index = jnp.arange(half_size, dtype=jnp.int32)
    inner_index = jnp.arange(inner_size, dtype=jnp.int32)
    first_angle = (
        2.0
        * math.pi
        / outer_size
        * (outer_index[:, None] * half_index[None, :] % outer_size).astype(jnp.float32)
    )
    twist_angle = (
        2.0
        * math.pi
        / full_size
        * (outer_index[:, None] * inner_index[None, :] % full_size).astype(jnp.float32)
    )
    last_angle = (
        2.0
        * math.pi
        / inner_size
        * (inner_index[:, None] * inner_index[None, :] % inner_size).astype(jnp.float32)
    )
    return (
        jnp.cos(first_angle),
        jnp.sin(first_angle),
        jnp.cos(twist_angle),
        jnp.sin(twist_angle),
        jnp.cos(last_angle),
        jnp.sin(last_angle),
    )


def forward(signal, tables):
    cos_first, sin_first, cos_twist, sin_twist, cos_last, sin_last = tables
    half_size = cos_first.shape[1]
    signal_grid = signal.reshape(signal.shape[0], half_size, 128)
    real_first = jnp.einsum("kn,rnm->rkm", cos_first, signal_grid, precision=full_precision)
    imag_first = -jnp.einsum("kn,rnm->rkm", sin_first, signal_grid, precision=full_precision)
    real_twist = real_first * cos_twist + imag_first * sin_twist
    imag_twist = imag_first * cos_twist - real_first * sin_twist
    real_last = jnp.einsum(
        "rkm,mj->rkj", real_twist, cos_last, precision=full_precision
    ) + jnp.einsum("rkm,mj->rkj", imag_twist, sin_last, precision=full_precision)
    imag_last = jnp.einsum(
        "rkm,mj->rkj", imag_twist, cos_last, precision=full_precision
    ) - jnp.einsum("rkm,mj->rkj", real_twist, sin_last, precision=full_precision)
    return (real_last, imag_last)


def inverse(real_part, imag_part, tables):
    cos_first, sin_first, cos_twist, sin_twist, cos_last, sin_last = tables
    half_size = cos_first.shape[1]
    row_total = real_part.shape[0]
    real_inner = jnp.einsum(
        "rkj,jm->rkm", real_part, cos_last, precision=full_precision
    ) - jnp.einsum("rkj,jm->rkm", imag_part, sin_last, precision=full_precision)
    imag_inner = jnp.einsum(
        "rkj,jm->rkm", imag_part, cos_last, precision=full_precision
    ) + jnp.einsum("rkj,jm->rkm", real_part, sin_last, precision=full_precision)
    real_twist = real_inner * cos_twist - imag_inner * sin_twist
    imag_twist = imag_inner * cos_twist + real_inner * sin_twist
    result = jnp.einsum(
        "kn,rkm->rnm", cos_first, real_twist, precision=full_precision
    ) - jnp.einsum("kn,rkm->rnm", sin_first, imag_twist, precision=full_precision)
    return (result / (2.0 * half_size * 128)).reshape(row_total, half_size * 128)


def filter_block(items, tables):
    mixed_blk, weighted_blk, kernel = items
    batches, chan_width, seq_length = mixed_blk.shape
    row_count = batches * chan_width
    mixed_wide = mixed_blk.astype(jnp.float32)
    weighted_wide = weighted_blk.astype(jnp.float32)
    stacked = jnp.concatenate(
        [
            mixed_wide.reshape(row_count, seq_length),
            weighted_wide.reshape(row_count, seq_length),
            kernel,
        ],
        axis=0,
    )
    real_spec, imag_spec = forward(stacked, tables)
    grid_shape = real_spec.shape[1:]
    mixed_real = real_spec[:row_count].reshape((batches, chan_width) + grid_shape)
    mixed_imag = imag_spec[:row_count].reshape((batches, chan_width) + grid_shape)
    weighted_real = real_spec[row_count : 2 * row_count].reshape((batches, chan_width) + grid_shape)
    weighted_imag = imag_spec[row_count : 2 * row_count].reshape((batches, chan_width) + grid_shape)
    kernel_real = real_spec[2 * row_count :][None]
    kernel_imag = imag_spec[2 * row_count :][None]
    conv_real = mixed_real * kernel_real - mixed_imag * kernel_imag
    conv_imag = mixed_real * kernel_imag + mixed_imag * kernel_real
    corr_real = kernel_real * weighted_real + kernel_imag * weighted_imag
    corr_imag = kernel_real * weighted_imag - kernel_imag * weighted_real
    slope_real = jnp.sum(mixed_real * weighted_real + mixed_imag * weighted_imag, axis=0)
    slope_imag = jnp.sum(mixed_real * weighted_imag - mixed_imag * weighted_real, axis=0)
    spec_real = jnp.concatenate(
        [
            conv_real.reshape((row_count,) + grid_shape),
            corr_real.reshape((row_count,) + grid_shape),
            slope_real,
        ],
        axis=0,
    )
    spec_imag = jnp.concatenate(
        [
            conv_imag.reshape((row_count,) + grid_shape),
            corr_imag.reshape((row_count,) + grid_shape),
            slope_imag,
        ],
        axis=0,
    )
    result = inverse(spec_real, spec_imag, tables)
    conv_vals = result[:row_count].reshape(batches, chan_width, seq_length).astype(jnp.bfloat16)
    corr_vals = (
        result[row_count : 2 * row_count]
        .reshape(batches, chan_width, seq_length)
        .astype(jnp.bfloat16)
    )
    slope = result[2 * row_count :]
    return (conv_vals, corr_vals, slope)


def run_blocks(mixed_rows, weighted_rows, filter_part):
    batches, part_width, seq_length = mixed_rows.shape
    block_width = min(part_width, 8)
    block_count = part_width // block_width
    tables = dft_tables(seq_length)

    def stack_rows(arr):
        return jnp.moveaxis(arr.reshape(batches, block_count, block_width, seq_length), 1, 0)

    def unstack_rows(arr):
        return jnp.moveaxis(arr, 0, 1).reshape(batches, part_width, seq_length)

    def one_block(items):
        return filter_block(items, tables)

    items = (
        stack_rows(mixed_rows),
        stack_rows(weighted_rows),
        filter_part.reshape(block_count, block_width, seq_length),
    )
    conv_vals, corr_vals, slope = lax.map(one_block, items)
    return (unstack_rows(conv_vals), unstack_rows(corr_vals), slope.reshape(part_width, seq_length))


def on_device(query_proj, key_proj, value_proj, cotangent, long_filter, skip_gain):
    query_rows = query_proj[0].astype(jnp.float32)
    key_rows = key_proj[0].astype(jnp.float32)
    value_rows = value_proj[0].astype(jnp.float32)
    cot_rows = cotangent[0].astype(jnp.float32)
    local_length = query_proj.shape[1]
    chan_width = query_proj.shape[2]
    seq_count = lax.axis_size("seq")
    batch_count = lax.axis_size("dp")
    factor = (batch_count * seq_count * local_length) ** (-0.5)
    mixed = (key_rows * value_rows).astype(jnp.bfloat16)
    weighted = (cot_rows * query_rows).astype(jnp.bfloat16)
    mixed_wide = mixed.astype(jnp.float32)
    weighted_wide = weighted.astype(jnp.float32)
    gain_term = factor * jnp.sum(weighted_wide * mixed_wide, axis=0)
    grad_skip = lax.psum(gain_term, ("seq", "dp"))
    filter_share = lax.all_to_all(long_filter.T, "seq", split_axis=0, concat_axis=1, tiled=True)
    groups = seq_count * batch_count
    share_width = chan_width // groups
    mixed_cols, weighted_cols = (
        lax.all_to_all(mixed.T, ("seq", "dp"), split_axis=0, concat_axis=1, tiled=True),
        lax.all_to_all(weighted.T, ("seq", "dp"), split_axis=0, concat_axis=1, tiled=True),
    )

    def to_sequences(arr):
        arr = arr.reshape(share_width, seq_count, batch_count, local_length)
        return jnp.transpose(arr, (2, 0, 1, 3)).reshape(
            batch_count, share_width, seq_count * local_length
        )

    def to_pieces(arr):
        arr = arr.reshape(batch_count, share_width, seq_count, local_length)
        return jnp.transpose(arr, (1, 2, 0, 3)).reshape(share_width, groups * local_length)

    filter_part = lax.dynamic_slice_in_dim(
        filter_share, lax.axis_index("dp") * share_width, share_width, 0
    )
    conv_vals, corr_vals, slope = run_blocks(
        to_sequences(mixed_cols), to_sequences(weighted_cols), filter_part
    )
    conv_back, corr_back = (
        lax.all_to_all(
            to_pieces(conv_vals), ("seq", "dp"), split_axis=1, concat_axis=0, tiled=True
        ),
        lax.all_to_all(
            to_pieces(corr_vals), ("seq", "dp"), split_axis=1, concat_axis=0, tiled=True
        ),
    )
    slope_share = lax.all_gather(slope, "dp", axis=0, tiled=True)
    slope_rows = lax.all_to_all(slope_share, "seq", split_axis=1, concat_axis=0, tiled=True)
    grad_filter = factor * slope_rows.T
    conv_rows = conv_back.T.astype(jnp.float32)
    corr_rows = corr_back.T.astype(jnp.float32)
    signal = conv_rows + skip_gain[None, :] * mixed_wide
    output = (query_rows * signal).astype(jnp.bfloat16)
    grad_query = (cot_rows * signal).astype(jnp.bfloat16)
    back = corr_rows + skip_gain[None, :] * weighted_wide
    grad_key = (back * value_rows).astype(jnp.bfloat16)
    grad_value = (back * key_rows).astype(jnp.bfloat16)
    return (
        output[None],
        grad_query[None],
        grad_key[None],
        grad_value[None],
        grad_filter,
        grad_skip,
    )


def solution(mesh):
    return jax.shard_map(
        on_device,
        mesh=mesh,
        in_specs=(
            P("dp", "seq", "chan"),
            P("dp", "seq", "chan"),
            P("dp", "seq", "chan"),
            P("dp", "seq", "chan"),
            P("seq", "chan"),
            P("chan"),
        ),
        out_specs=(
            P("dp", "seq", "chan"),
            P("dp", "seq", "chan"),
            P("dp", "seq", "chan"),
            P("dp", "seq", "chan"),
            P("seq", "chan"),
            P("chan"),
        ),
        check_vma=False,
    )
```

profile of v0, /device:TPU:32, one launch (start us, length us, event | category | flops | bytes accessed | tf_op | source)
XLA Modules:
  0.0 319.2 jit_solution(15264044031151015225)
XLA Ops:
  11.3 22.9 %all_to_all.90 = bf16[16,32,512]{2,1,0:T(8,128)(2,1)S(1)} all-to-all(bf16[16,32,512]{2,1,0:T(8,128)(2,1)S(1)} %bitcast.249), channel_id=1, replica_groups=mesh['seq'=8,'chan'=16,'dp'=2] {'seq','dp'}, dimensions={0} | all-to-all | bytes 1048576 | tf_op jit(solution)/shard_map/all_to_all | solution.py:181
  34.1 5.7 %all-to-all-start = ((bf16[16,32,512]{2,1,0:T(8,128)(2,1)}), bf16[16,32,512]{2,1,0:T(8,128)(2,1)S(1)}, u32[]{:S(2)}, u32[]{:S(2)}) async-start(bf16[16,32,512]{2,1,0:T(8,128)(2,1)} %bitcast.4), calls=%async_computation | async-start | bytes 1048576 | tf_op jit(solution)/shard_map/all_to_all | solution.py:180
  41.2 13.2 %all-to-all-done = bf16[16,32,512]{2,1,0:T(8,128)(2,1)S(1)} async-done(((bf16[16,32,512]{2,1,0:T(8,128)(2,1)}), bf16[16,32,512]{2,1,0:T(8,128)(2,1)S(1)}, u32[]{:S(2)}, u32[]{:S(2)}) %all-to-all-start) | async-done | bytes 524320 | tf_op jit(solution)/shard_map/all_to_all | solution.py:180
  54.4 4.8 %all-to-all-start.2 = ((f32[8,64,512]{2,1,0:T(8,128)}), f32[8,64,512]{2,1,0:T(8,128)S(1)}, u32[]{:S(2)}, u32[]{:S(2)}) async-start(f32[8,64,512]{2,1,0:T(8,128)} %bitcast.18), calls=%async_computation.2 | async-start | bytes 2097152 | tf_op jit(solution)/shard_map/all_to_all | solution.py:176
  61.9 26.4 %all-to-all-done.2 = f32[8,64,512]{2,1,0:T(8,128)S(1)} async-done(((f32[8,64,512]{2,1,0:T(8,128)}), f32[8,64,512]{2,1,0:T(8,128)S(1)}, u32[]{:S(2)}, u32[]{:S(2)}) %all-to-all-start.2) | async-done | bytes 1048608 | tf_op jit(solution)/shard_map/all_to_all | solution.py:176
  89.3 108.2 %while.16 = (s32[]{:T(128)}, bf16[4,2,8,4096]{3,2,1,0:T(8,128)(2,1)}, bf16[4,2,8,4096]{3,2,1,0:T(8,128)(2,1)}, f32[4,8,4096]{2,1,0:T(8,128)}, bf16[4,2,8,4096]{3...) while((s32[]{:T(128)}, ...), condition=%wide.region_3.4_spmd.clone.clone, body=%wide.region_0.3_spmd.clone.clone.sunk | while | flops 4545183744 | bytes 59639460 | solution.py:156
  102.2 2.4 fusion.201
  104.6 1.8 reduce_sum.35
  106.4 2.5 convolution_add_fusion.5
  129.3 2.4 fusion.201
  133.5 2.5 convolution_add_fusion.5
  156.3 2.4 fusion.201
  160.5 2.5 convolution_add_fusion.5
  183.3 2.4 fusion.201
  187.6 2.5 convolution_add_fusion.5
  199.7 4.5 %all-to-all-start.3 = ((bf16[32,16,512]{2,0,1:T(8,128)(2,1)}), bf16[32,16,512]{2,0,1:T(8,128)(2,1)S(1)}, u32[]{:S(2)}, u32[]{:S(2)}) async-start(bf16[32,16,512]{2,0,1:T(8,128)(2,1)} %bitcast.23), calls=%async_computation.3 | async-start | bytes 1048576 | tf_op jit(solution)/shard_map/all_to_all | solution.py:201
  205.9 12.8 %all-to-all-done.3 = bf16[32,16,512]{2,0,1:T(8,128)(2,1)S(1)} async-done(((bf16[32,16,512]{2,0,1:T(8,128)(2,1)}), bf16[32,16,512]{2,0,1:T(8,128)(2,1)S(1)}, u32[]{:S(2)}, u32[]{:S(2)}) %all-to-all-start.3) | async-done | bytes 524320 | tf_op jit(solution)/shard_map/all_to_all | solution.py:201
  218.7 5.8 %all-to-all-start.4 = ((bf16[32,16,512]{2,0,1:T(8,128)(2,1)}), bf16[32,16,512]{2,0,1:T(8,128)(2,1)}, u32[]{:S(2)}, u32[]{:S(2)}) async-start(bf16[32,16,512]{2,0,1:T(8,128)(2,1)} %bitcast.32), calls=%async_computation.4 | async-start | bytes 1048576 | tf_op jit(solution)/shard_map/all_to_all | solution.py:204
  224.5 19.5 %all-gather.2.cloned.1.call-done = f32[64,4096]{1,0:T(8,128)} async-done(((f32[32,4096]{1,0:T(8,128)}), f32[64,4096]{1,0:T(8,128)}) %all-gather.2.cloned.1.call-update) | async-done | bytes 1048592 | tf_op jit(solution)/shard_map/all_gather | solution.py:208
  244.0 2.3 copy.83
  246.4 7.9 %all-to-all-start.5 = ((f32[64,8,512]{2,0,1:T(8,128)}), f32[64,8,512]{2,0,1:T(8,128)}, u32[]{:S(2)}, u32[]{:S(2)}) async-start(f32[64,8,512]{2,0,1:T(8,128)} %bitcast.251), calls=%async_computation.5 | async-start | bytes 2097152 | tf_op jit(solution)/shard_map/all_to_all | solution.py:209
  254.3 47.0 %psum.7 = f32[512]{0:T(512)} all-reduce(f32[512]{0:T(512)S(1)} %broadcast_multiply_fusion.1), channel_id=1, replica_groups=mesh['seq'=8,'chan'=16,'dp'=2] {'seq','dp'}, use_global_device_ids=true, to_apply=%region_5.6 | all-reduce | flops 512 | bytes 4096 | tf_op jit(solution)/shard_map/psum | solution.py:175
  301.3 3.2 %fusion.150 = (bf16[512,512]{0,1:T(8,128)(2,1)}, bf16[512,512]{0,1:T(8,128)(2,1)}, bf16[512,512]{0,1:T(8,128)(2,1)}, bf16[512,512]{0,1:T(8,128)(2,1)}) fusion(bf16[512,512]{0,1:T(8,128)(2,1)S(1)} %copy-done.11, bf16[32,16,512]{2,0,1:T(8,128)(2,1)} %all-to-all-done.4, bf16[1,512,512]{1,2,0:T(8,128)(2,1)S(1)} %copy-done.5, f32[512]{0:T(512)S(1)} %copy-done.20, ...), kind=kLoop, calls=%fused_computation.173 | loop fusion | flops 5242880 | bytes 6293504 | tf_op jit(solution)/shard_map/convert_element_type | solution.py:218
  304.6 2.1 copy.65
  (210 shorter events, 104.6 us)
Async XLA Ops:
  7.2 1.6 copy-start.17
  7.2 1.9 copy-start.18
  8.8 1.7 copy-start.4
  10.5 29.4 %copy-start.15 = (f32[512,512]{1,0:T(8,128)S(1)}, f32[512,512]{1,0:T(8,128)}, u32[]{:S(2)}) copy-start(f32[512,512]{1,0:T(8,128)} %param.12) | copy-start | bytes 3145732
  34.1 20.2 %all-to-all-start = ((bf16[16,32,512]{2,1,0:T(8,128)(2,1)}), bf16[16,32,512]{2,1,0:T(8,128)(2,1)S(1)}, u32[]{:S(2)}, u32[]{:S(2)}) async-start(bf16[16,32,512]{2,1,0:T(8,128)(2,1)} %bitcast.4), calls=%async_computation | async-start | bytes 1048576 | tf_op jit(solution)/shard_map/all_to_all | solution.py:180
  54.4 34.0 %all-to-all-start.2 = ((f32[8,64,512]{2,1,0:T(8,128)}), f32[8,64,512]{2,1,0:T(8,128)S(1)}, u32[]{:S(2)}, u32[]{:S(2)}) async-start(f32[8,64,512]{2,1,0:T(8,128)} %bitcast.18), calls=%async_computation.2 | async-start | bytes 2097152 | tf_op jit(solution)/shard_map/all_to_all | solution.py:176
  106.4 2.5 copy-start.1
  133.5 2.5 copy-start.1
  160.5 2.5 copy-start.1
  187.5 2.5 copy-start.1
  198.8 5.5 %copy-start.19 = (bf16[4,2,8,4096]{3,2,1,0:T(8,128)(2,1)S(1)}, bf16[4,2,8,4096]{3,2,1,0:T(8,128)(2,1)}, u32[]{:S(2)}) copy-start(bf16[4,2,8,4096]{3,2,1,0:T(8,128)(2,1)} %get-tuple-element.118) | copy-start | bytes 1572868
  199.7 19.0 %all-to-all-start.3 = ((bf16[32,16,512]{2,0,1:T(8,128)(2,1)}), bf16[32,16,512]{2,0,1:T(8,128)(2,1)S(1)}, u32[]{:S(2)}, u32[]{:S(2)}) async-start(bf16[32,16,512]{2,0,1:T(8,128)(2,1)} %bitcast.23), calls=%async_computation.3 | async-start | bytes 1048576 | tf_op jit(solution)/shard_map/all_to_all | solution.py:201
  204.2 39.8 %all-gather.2.cloned.1.call-start = ((), (), s32[]{:S(2)}) async-start(), calls=%async_computation.6 | async-start | bytes 1572864 | tf_op jit(solution)/shard_map/all_gather | solution.py:208
  218.7 27.7 %all-to-all-start.4 = ((bf16[32,16,512]{2,0,1:T(8,128)(2,1)}), bf16[32,16,512]{2,0,1:T(8,128)(2,1)}, u32[]{:S(2)}, u32[]{:S(2)}) async-start(bf16[32,16,512]{2,0,1:T(8,128)(2,1)} %bitcast.32), calls=%async_computation.4 | async-start | bytes 1048576 | tf_op jit(solution)/shard_map/all_to_all | solution.py:204
  244.0 57.3 %copy-start.11 = (bf16[512,512]{0,1:T(8,128)(2,1)S(1)}, bf16[512,512]{0,1:T(8,128)(2,1)}, u32[]{:S(2)}) copy-start(bf16[512,512]{0,1:T(8,128)(2,1)} %copy-done.10) | copy-start | bytes 1572868
  246.3 55.0 %copy-start.3 = (bf16[1,512,512]{1,2,0:T(8,128)(2,1)S(1)}, bf16[1,512,512]{1,2,0:T(8,128)(2,1)}, u32[]{:S(2)}) copy-start(bf16[1,512,512]{1,2,0:T(8,128)(2,1)} %copy-done.2) | copy-start | bytes 1572868
  246.3 55.0 %copy-start.5 = (bf16[1,512,512]{1,2,0:T(8,128)(2,1)S(1)}, bf16[1,512,512]{1,2,0:T(8,128)(2,1)}, u32[]{:S(2)}) copy-start(bf16[1,512,512]{1,2,0:T(8,128)(2,1)} %copy-done.4) | copy-start | bytes 1572868
  246.4 55.0 %copy-start.7 = (bf16[1,512,512]{1,2,0:T(8,128)(2,1)S(1)}, bf16[1,512,512]{1,2,0:T(8,128)(2,1)}, u32[]{:S(2)}) copy-start(bf16[1,512,512]{1,2,0:T(8,128)(2,1)} %copy-done.6) | copy-start | bytes 1572868
  246.4 55.0 %copy-start.9 = (bf16[1,512,512]{1,2,0:T(8,128)(2,1)S(1)}, bf16[1,512,512]{1,2,0:T(8,128)(2,1)}, u32[]{:S(2)}) copy-start(bf16[1,512,512]{1,2,0:T(8,128)(2,1)} %copy-done.8) | copy-start | bytes 1572868
  246.4 55.0 %copy-start.20 = (f32[512]{0:T(512)S(1)}, f32[512]{0:T(512)}, u32[]{:S(2)}) copy-start(f32[512]{0:T(512)} %param.13) | copy-start | bytes 6148
  246.4 63.3 %all-to-all-start.5 = ((f32[64,8,512]{2,0,1:T(8,128)}), f32[64,8,512]{2,0,1:T(8,128)}, u32[]{:S(2)}, u32[]{:S(2)}) async-start(f32[64,8,512]{2,0,1:T(8,128)} %bitcast.251), calls=%async_computation.5 | async-start | bytes 2097152 | tf_op jit(solution)/shard_map/all_to_all | solution.py:209
  304.6 2.1 copy-start.14
  304.6 3.1 copy-start.13
  306.7 2.0 copy-start.12
  (9 other events, 11.4 us)
Sparse Core Ops, SparseCore 0:
  206.8 37.1 all-gather.1
where the time goes:
time: 321 us; the launch traced here: 319 us
  matrix products  74.1 us (23%)
  waiting for transfers between devices  72.4 us (23%)
  blocking collectives  69.9 us (22%)
  local copies, waits for them, and re-layouts  33.4 us (10%)
  starting transfers between devices  28.7 us (9%)
  other arithmetic  25.6 us (8%)
  between operations  14.3 us (4%)
    psum x1, blocking collectives, on_device(): grad_skip = lax.psum(gain_term, ('seq', 'dp'))  47 us
    all_to_all x1, waiting for transfers between devices, on_device(): lax.all_to_all(long_filter.T, 'seq', split_axis=0, concat_axis=1, tiled=T...  26.4 us
    all_to_all x1, blocking collectives, on_device(): lax.all_to_all(weighted.T, ('seq', 'dp'), split_axis=0, concat_axis=1, ti...  22.9 us
    all_gather x1, waiting for transfers between devices, on_device(): slope_share = lax.all_gather(slope, 'dp', axis=0, tiled=True)  19.5 us
    all_to_all x1, waiting for transfers between devices, on_device(): lax.all_to_all(mixed.T, ('seq', 'dp'), split_axis=0, concat_axis=1, tiled...  13.2 us
    all_to_all x1, waiting for transfers between devices, on_device(): lax.all_to_all(to_pieces(conv_vals), ('seq', 'dp'), split_axis=1, concat_...  12.8 us
    unnamed x50, local copies, waits for them, and re-layouts  11.1 us
    dot_general x4, matrix products, inverse(): jnp.einsum('rkj,jm->rkm', real_part, sin_last, precision=full_precision)  9.98 us
  transfers between devices with their start and end apart: 6, of which 4 were waited for; matrix products, arithmetic and copies ran while one was open for 5% of the time, Pallas kernels for 0%

commit v1 on v0

--- a/solution.py
+++ b/solution.py
@@ -172,7 +172,7 @@
     mixed_wide = mixed.astype(jnp.float32)
     weighted_wide = weighted.astype(jnp.float32)
     gain_term = factor * jnp.sum(weighted_wide * mixed_wide, axis=0)
-    grad_skip = lax.psum(gain_term, ("seq", "dp"))
+    grad_skip = lax.psum(lax.psum(gain_term, "seq"), "dp")
     filter_share = lax.all_to_all(long_filter.T, "seq", split_axis=0, concat_axis=1, tiled=True)
     groups = seq_count * batch_count
     share_width = chan_width // groups

time: 321 us -> 315 us (0.981)
  blocking collectives: 69.9 us -> 64 us
    psum x1 -> x2, blocking collectives: 47 us -> 41.2 us  [on_device(): grad_skip = lax.psum(lax.psum(gain_term, 'seq'), 'dp')]
where the time goes in v1:
time: 315 us; the launch traced here: 313 us
  matrix products  74.1 us (24%)
  waiting for transfers between devices  72.4 us (23%)
  blocking collectives  64 us (20%)
  local copies, waits for them, and re-layouts  33.4 us (11%)
  starting transfers between devices  28.7 us (9%)
  other arithmetic  25.4 us (8%)
  between operations  14.3 us (5%)
    psum x2, blocking collectives, on_device(): grad_skip = lax.psum(lax.psum(gain_term, 'seq'), 'dp')  41.2 us
    all_to_all x1, waiting for transfers between devices, on_device(): lax.all_to_all(long_filter.T, 'seq', split_axis=0, concat_axis=1, tiled=T...  26.4 us
    all_to_all x1, blocking collectives, on_device(): lax.all_to_all(weighted.T, ('seq', 'dp'), split_axis=0, concat_axis=1, ti...  22.9 us
    all_gather x1, waiting for transfers between devices, on_device(): slope_share = lax.all_gather(slope, 'dp', axis=0, tiled=True)  19.5 us
    all_to_all x1, waiting for transfers between devices, on_device(): lax.all_to_all(mixed.T, ('seq', 'dp'), split_axis=0, concat_axis=1, tiled...  13.2 us
    all_to_all x1, waiting for transfers between devices, on_device(): lax.all_to_all(to_pieces(conv_vals), ('seq', 'dp'), split_axis=1, concat_...  12.8 us
    unnamed x50, local copies, waits for them, and re-layouts  11.1 us
    dot_general x4, matrix products, inverse(): jnp.einsum('rkj,jm->rkm', real_part, sin_last, precision=full_precision)  10 us
  transfers between devices with their start and end apart: 6, of which 4 were waited for; matrix products, arithmetic and copies ran while one was open for 5% of the time, Pallas kernels for 0%

profile of v1, /device:TPU:32, one launch (start us, length us, event | category | flops | bytes accessed | tf_op | source)
XLA Modules:
  0.0 313.2 jit_solution(14485106665526045109)
XLA Ops:
  11.3 22.9 %all_to_all.90 = bf16[16,32,512]{2,1,0:T(8,128)(2,1)S(1)} all-to-all(bf16[16,32,512]{2,1,0:T(8,128)(2,1)S(1)} %bitcast.249), channel_id=1, replica_groups=mesh['seq'=8,'chan'=16,'dp'=2] {'seq','dp'}, dimensions={0} | all-to-all | bytes 1048576 | tf_op jit(solution)/shard_map/all_to_all | solution.py:181
  34.1 5.7 %all-to-all-start = ((bf16[16,32,512]{2,1,0:T(8,128)(2,1)}), bf16[16,32,512]{2,1,0:T(8,128)(2,1)S(1)}, u32[]{:S(2)}, u32[]{:S(2)}) async-start(bf16[16,32,512]{2,1,0:T(8,128)(2,1)} %bitcast.4), calls=%async_computation | async-start | bytes 1048576 | tf_op jit(solution)/shard_map/all_to_all | solution.py:180
  41.2 13.2 %all-to-all-done = bf16[16,32,512]{2,1,0:T(8,128)(2,1)S(1)} async-done(((bf16[16,32,512]{2,1,0:T(8,128)(2,1)}), bf16[16,32,512]{2,1,0:T(8,128)(2,1)S(1)}, u32[]{:S(2)}, u32[]{:S(2)}) %all-to-all-start) | async-done | bytes 524320 | tf_op jit(solution)/shard_map/all_to_all | solution.py:180
  54.4 4.8 %all-to-all-start.2 = ((f32[8,64,512]{2,1,0:T(8,128)}), f32[8,64,512]{2,1,0:T(8,128)S(1)}, u32[]{:S(2)}, u32[]{:S(2)}) async-start(f32[8,64,512]{2,1,0:T(8,128)} %bitcast.18), calls=%async_computation.2 | async-start | bytes 2097152 | tf_op jit(solution)/shard_map/all_to_all | solution.py:176
  61.9 26.4 %all-to-all-done.2 = f32[8,64,512]{2,1,0:T(8,128)S(1)} async-done(((f32[8,64,512]{2,1,0:T(8,128)}), f32[8,64,512]{2,1,0:T(8,128)S(1)}, u32[]{:S(2)}, u32[]{:S(2)}) %all-to-all-start.2) | async-done | bytes 1048608 | tf_op jit(solution)/shard_map/all_to_all | solution.py:176
  89.3 108.0 %while.16 = (s32[]{:T(128)}, bf16[4,2,8,4096]{3,2,1,0:T(8,128)(2,1)}, bf16[4,2,8,4096]{3,2,1,0:T(8,128)(2,1)}, f32[4,8,4096]{2,1,0:T(8,128)}, bf16[4,2,8,4096]{3...) while((s32[]{:T(128)}, ...), condition=%wide.region_3.4_spmd.clone.clone, body=%wide.region_0.3_spmd.clone.clone.sunk | while | flops 4545183744 | bytes 59639460 | solution.py:156
  102.2 2.4 fusion.201
  106.4 2.5 convolution_add_fusion.5
  129.2 2.4 fusion.201
  133.4 2.5 convolution_add_fusion.5
  156.2 2.4 fusion.201
  160.4 2.5 convolution_add_fusion.5
  183.2 2.4 fusion.201
  187.4 2.5 convolution_add_fusion.5
  199.5 4.5 %all-to-all-start.3 = ((bf16[32,16,512]{2,0,1:T(8,128)(2,1)}), bf16[32,16,512]{2,0,1:T(8,128)(2,1)S(1)}, u32[]{:S(2)}, u32[]{:S(2)}) async-start(bf16[32,16,512]{2,0,1:T(8,128)(2,1)} %bitcast.23), calls=%async_computation.3 | async-start | bytes 1048576 | tf_op jit(solution)/shard_map/all_to_all | solution.py:201
  205.7 12.8 %all-to-all-done.3 = bf16[32,16,512]{2,0,1:T(8,128)(2,1)S(1)} async-done(((bf16[32,16,512]{2,0,1:T(8,128)(2,1)}), bf16[32,16,512]{2,0,1:T(8,128)(2,1)S(1)}, u32[]{:S(2)}, u32[]{:S(2)}) %all-to-all-start.3) | async-done | bytes 524320 | tf_op jit(solution)/shard_map/all_to_all | solution.py:201
  218.5 5.8 %all-to-all-start.4 = ((bf16[32,16,512]{2,0,1:T(8,128)(2,1)}), bf16[32,16,512]{2,0,1:T(8,128)(2,1)}, u32[]{:S(2)}, u32[]{:S(2)}) async-start(bf16[32,16,512]{2,0,1:T(8,128)(2,1)} %bitcast.32), calls=%async_computation.4 | async-start | bytes 1048576 | tf_op jit(solution)/shard_map/all_to_all | solution.py:204
  224.3 19.5 %all-gather.2.cloned.1.call-done = f32[64,4096]{1,0:T(8,128)} async-done(((f32[32,4096]{1,0:T(8,128)}), f32[64,4096]{1,0:T(8,128)}) %all-gather.2.cloned.1.call-update) | async-done | bytes 1048592 | tf_op jit(solution)/shard_map/all_gather | solution.py:208
  243.8 2.3 copy.83
  246.2 7.9 %all-to-all-start.5 = ((f32[64,8,512]{2,0,1:T(8,128)}), f32[64,8,512]{2,0,1:T(8,128)}, u32[]{:S(2)}, u32[]{:S(2)}) async-start(f32[64,8,512]{2,0,1:T(8,128)} %bitcast.250), calls=%async_computation.5 | async-start | bytes 2097152 | tf_op jit(solution)/shard_map/all_to_all | solution.py:209
  254.1 35.7 %psum.14 = f32[512]{0:T(512)S(1)} all-reduce(f32[512]{0:T(512)S(1)} %broadcast_multiply_fusion.1), channel_id=1, replica_groups=mesh['seq'=8,'chan'=16,'dp'=2] {'seq'}, use_global_device_ids=true, to_apply=%region_5.6 | all-reduce | flops 512 | bytes 4096 | tf_op jit(solution)/shard_map/psum | solution.py:175
  289.8 5.5 %psum.15 = f32[512]{0:T(512)} all-reduce(f32[512]{0:T(512)S(1)} %psum.14), channel_id=1, replica_groups=mesh['seq'=8,'chan'=16,'dp'=2] {'dp'}, use_global_device_ids=true, to_apply=%region_6.7 | all-reduce | flops 512 | bytes 4096 | tf_op jit(solution)/shard_map/psum | solution.py:175
  295.3 3.2 %fusion.150 = (bf16[512,512]{0,1:T(8,128)(2,1)}, bf16[512,512]{0,1:T(8,128)(2,1)}, bf16[512,512]{0,1:T(8,128)(2,1)}, bf16[512,512]{0,1:T(8,128)(2,1)}) fusion(bf16[512,512]{0,1:T(8,128)(2,1)S(1)} %copy-done.11, bf16[32,16,512]{2,0,1:T(8,128)(2,1)} %all-to-all-done.4, bf16[1,512,512]{1,2,0:T(8,128)(2,1)S(1)} %copy-done.5, f32[512]{0:T(512)S(1)} %copy-done.20, ...), kind=kLoop, calls=%fused_computation.173 | loop fusion | flops 5242880 | bytes 6293504 | tf_op jit(solution)/shard_map/convert_element_type | solution.py:218
  298.5 2.1 copy.65
  (211 shorter events, 106.2 us)
Async XLA Ops:
  7.2 1.6 copy-start.17
  7.2 1.9 copy-start.18
  8.8 1.7 copy-start.4
  10.5 29.4 %copy-start.15 = (f32[512,512]{1,0:T(8,128)S(1)}, f32[512,512]{1,0:T(8,128)}, u32[]{:S(2)}) copy-start(f32[512,512]{1,0:T(8,128)} %param.12) | copy-start | bytes 3145732
  34.1 20.2 %all-to-all-start = ((bf16[16,32,512]{2,1,0:T(8,128)(2,1)}), bf16[16,32,512]{2,1,0:T(8,128)(2,1)S(1)}, u32[]{:S(2)}, u32[]{:S(2)}) async-start(bf16[16,32,512]{2,1,0:T(8,128)(2,1)} %bitcast.4), calls=%async_computation | async-start | bytes 1048576 | tf_op jit(solution)/shard_map/all_to_all | solution.py:180
  54.4 34.0 %all-to-all-start.2 = ((f32[8,64,512]{2,1,0:T(8,128)}), f32[8,64,512]{2,1,0:T(8,128)S(1)}, u32[]{:S(2)}, u32[]{:S(2)}) async-start(f32[8,64,512]{2,1,0:T(8,128)} %bitcast.18), calls=%async_computation.2 | async-start | bytes 2097152 | tf_op jit(solution)/shard_map/all_to_all | solution.py:176
  106.4 2.5 copy-start.1
  133.4 2.5 copy-start.1
  160.3 2.5 copy-start.1
  187.3 2.5 copy-start.1
  198.6 5.5 %copy-start.19 = (bf16[4,2,8,4096]{3,2,1,0:T(8,128)(2,1)S(1)}, bf16[4,2,8,4096]{3,2,1,0:T(8,128)(2,1)}, u32[]{:S(2)}) copy-start(bf16[4,2,8,4096]{3,2,1,0:T(8,128)(2,1)} %get-tuple-element.118) | copy-start | bytes 1572868
  199.5 19.0 %all-to-all-start.3 = ((bf16[32,16,512]{2,0,1:T(8,128)(2,1)}), bf16[32,16,512]{2,0,1:T(8,128)(2,1)S(1)}, u32[]{:S(2)}, u32[]{:S(2)}) async-start(bf16[32,16,512]{2,0,1:T(8,128)(2,1)} %bitcast.23), calls=%async_computation.3 | async-start | bytes 1048576 | tf_op jit(solution)/shard_map/all_to_all | solution.py:201
  204.0 39.8 %all-gather.2.cloned.1.call-start = ((), (), s32[]{:S(2)}) async-start(), calls=%async_computation.6 | async-start | bytes 1572864 | tf_op jit(solution)/shard_map/all_gather | solution.py:208
  218.5 27.7 %all-to-all-start.4 = ((bf16[32,16,512]{2,0,1:T(8,128)(2,1)}), bf16[32,16,512]{2,0,1:T(8,128)(2,1)}, u32[]{:S(2)}, u32[]{:S(2)}) async-start(bf16[32,16,512]{2,0,1:T(8,128)(2,1)} %bitcast.32), calls=%async_computation.4 | async-start | bytes 1048576 | tf_op jit(solution)/shard_map/all_to_all | solution.py:204
  243.8 51.5 %copy-start.11 = (bf16[512,512]{0,1:T(8,128)(2,1)S(1)}, bf16[512,512]{0,1:T(8,128)(2,1)}, u32[]{:S(2)}) copy-start(bf16[512,512]{0,1:T(8,128)(2,1)} %copy-done.10) | copy-start | bytes 1572868
  246.1 49.1 %copy-start.3 = (bf16[1,512,512]{1,2,0:T(8,128)(2,1)S(1)}, bf16[1,512,512]{1,2,0:T(8,128)(2,1)}, u32[]{:S(2)}) copy-start(bf16[1,512,512]{1,2,0:T(8,128)(2,1)} %copy-done.2) | copy-start | bytes 1572868
  246.1 49.1 %copy-start.5 = (bf16[1,512,512]{1,2,0:T(8,128)(2,1)S(1)}, bf16[1,512,512]{1,2,0:T(8,128)(2,1)}, u32[]{:S(2)}) copy-start(bf16[1,512,512]{1,2,0:T(8,128)(2,1)} %copy-done.4) | copy-start | bytes 1572868
  246.1 49.1 %copy-start.7 = (bf16[1,512,512]{1,2,0:T(8,128)(2,1)S(1)}, bf16[1,512,512]{1,2,0:T(8,128)(2,1)}, u32[]{:S(2)}) copy-start(bf16[1,512,512]{1,2,0:T(8,128)(2,1)} %copy-done.6) | copy-start | bytes 1572868
  246.2 49.1 %copy-start.9 = (bf16[1,512,512]{1,2,0:T(8,128)(2,1)S(1)}, bf16[1,512,512]{1,2,0:T(8,128)(2,1)}, u32[]{:S(2)}) copy-start(bf16[1,512,512]{1,2,0:T(8,128)(2,1)} %copy-done.8) | copy-start | bytes 1572868
  246.2 49.2 %copy-start.20 = (f32[512]{0:T(512)S(1)}, f32[512]{0:T(512)}, u32[]{:S(2)}) copy-start(f32[512]{0:T(512)} %param.13) | copy-start | bytes 6148
  246.2 57.5 %all-to-all-start.5 = ((f32[64,8,512]{2,0,1:T(8,128)}), f32[64,8,512]{2,0,1:T(8,128)}, u32[]{:S(2)}, u32[]{:S(2)}) async-start(f32[64,8,512]{2,0,1:T(8,128)} %bitcast.250), calls=%async_computation.5 | async-start | bytes 2097152 | tf_op jit(solution)/shard_map/all_to_all | solution.py:209
  298.5 2.1 copy-start.14
  298.5 3.1 %copy-start.13 = (bf16[512,512]{0,1:T(8,128)(2,1)S(1)}, bf16[512,512]{0,1:T(8,128)(2,1)}, u32[]{:S(2)}) copy-start(bf16[512,512]{0,1:T(8,128)(2,1)} %get-tuple-element.265) | copy-start | bytes 1572868
  300.7 2.0 copy-start.12
  (9 other events, 11.4 us)
Sparse Core Ops, SparseCore 0:
  206.6 37.1 all-gather.1
